TPU v7x, 512 devices: a whole 4x8x8 slice. The times are simulated.
512 devices in a mesh: seq: 128 (over x, z_hi, y, core), tp: 4 (over z_lo).
Axes of the slice: x: 4, y: 8, z: 8 (z_hi: 2, z_lo: 4; z = z_hi * 4 + z_lo), core: 2. Of those that a mesh axis runs over, the one named last changes fastest.
Arguments:
- queries: bfloat16 [16384, 4096], P('seq', 'tp'), may hold values from -6 to 6
- suffix_entries: bfloat16 [16384, 4096], P('seq', 'tp'), may hold values from -6 to 6
- prefix_cache: bfloat16 [2048, 4096], P(('seq', 'tp')), may hold values from -6 to 6
- block_prefix: int32 [512], replicated, may hold values from 0 to 1, as said below
- request_lengths: int32 [512], P('seq'), may hold values from 0 to 128, as said below
- request_prefix: int32 [512], P('seq'), may hold values from 0 to 1
Outputs:
- attended: bfloat16 [16384, 4096], P('seq', 'tp')
Inputs may be any that keep to these rules, and one draw needn't show every extreme that they name: `request_lengths`: the lengths of one index of seq's requests sum to at most 128; at some index they sum to exactly 128, and there one request alone takes all 128 slots. `block_prefix`: exactly half of the blocks belong to each prefix.
All inputs are finite; a program needn't handle non-finite values.
Results may differ from a plain program's by a relative error of at most 0.0049.
Values may be sent and summed in bfloat16 or wider, within the bound.
No kernel may reach another device: no remote copies, remote signals or barrier semaphores. Data moves between devices by JAX's collectives and lax.ppermute only.
A program may use at most 64 MiB of HBM per device.

v0:
```python
import math
import jax
import jax.numpy as jnp
from jax import lax
from jax.sharding import PartitionSpec as P

HEADS = 16
HEAD = 128
masked_score = -1e30
section_rows = 512


def token_layout(lengths, prefixes, slots):
    cumulative = jnp.cumsum(lengths)
    slot_ids = jnp.arange(slots, dtype=jnp.int32)
    request_ids = jnp.sum((slot_ids[:, None] >= cumulative[None, :]).astype(jnp.int32), axis=1)
    live_slots = slot_ids < cumulative[-1]
    onehot = request_ids[:, None] == jnp.arange(lengths.shape[0], dtype=jnp.int32)[None, :]
    token_group = jnp.sum(jnp.where(onehot, prefixes[None, :], 0), axis=1)
    return (slot_ids, request_ids, live_slots, token_group)


def attend(running, query_rows, key_rows, value_rows, allowed):
    old_max, old_total, old_sum = running
    scores = jnp.einsum("thed,rhd->ther", query_rows, key_rows, preferred_element_type=jnp.float32)
    scores = scores * (1.0 / math.sqrt(query_rows.shape[-1]))
    allowed_grid = allowed[:, None, None, :]
    scores = jnp.where(allowed_grid, scores, masked_score)
    new_max = jnp.maximum(old_max, jnp.max(scores, axis=-1))
    rescale = jnp.exp(old_max - new_max)
    weights = jnp.where(allowed_grid, jnp.exp(scores - new_max[..., None]), 0.0)
    new_total = old_total * rescale + jnp.sum(weights, axis=-1)
    products = jnp.einsum(
        "ther,rhd->thed",
        weights.astype(jnp.bfloat16),
        value_rows,
        preferred_element_type=jnp.float32,
    )
    new_sum = old_sum * rescale[..., None] + products
    return (new_max, new_total, new_sum)


def owner_lookup(block_ids, block_prefix):
    match = block_ids[:, None] == jnp.arange(block_prefix.shape[0], dtype=jnp.int32)[None, :]
    return jnp.sum(jnp.where(match, block_prefix[None, :], 0), axis=1)


def empty_state(token_rows, head_count):
    return (
        jnp.full((token_rows, head_count, 2), masked_score, jnp.float32),
        jnp.zeros((token_rows, head_count, 2), jnp.float32),
        jnp.zeros((token_rows, head_count, 2, HEAD), jnp.float32),
    )


def sweep(running, query_rows, rows, head_count, block_of, block_prefix, token_group, live_slots):
    total_rows = rows.shape[0]
    for offset in range(0, total_rows, section_rows):
        row_count = min(section_rows, total_rows - offset)
        section = rows[offset : offset + row_count].reshape(row_count, head_count, 2, HEAD)
        positions = offset + jnp.arange(row_count, dtype=jnp.int32)
        owners = owner_lookup(block_of(positions), block_prefix)
        allowed = (token_group[:, None] == owners[None, :]) & live_slots[:, None]
        running = attend(running, query_rows, section[:, :, 0], section[:, :, 1], allowed)
    return running


def per_device(
    queries, suffix_entries, prefix_cache, block_prefix, request_lengths, request_prefix
):
    tensor_count = lax.axis_size("tp")
    seq_count = lax.axis_size("seq")
    local_heads = HEADS // tensor_count
    token_rows = queries.shape[0]
    block_rows = prefix_cache.shape[0]
    slot_ids, request_ids, live_slots, token_group = token_layout(
        request_lengths, request_prefix, token_rows
    )
    own_query = queries.reshape(token_rows, local_heads, 2, HEAD)
    own_entries = suffix_entries.reshape(token_rows, local_heads, 2, HEAD)
    gathered = lax.all_gather(prefix_cache, "seq", axis=0, tiled=True)
    cached = lax.all_to_all(gathered, "tp", split_axis=1, concat_axis=0, tiled=True)
    span = seq_count * block_rows

    def block_of(positions):
        return positions % span // block_rows * tensor_count + positions // span

    running = sweep(
        empty_state(token_rows, local_heads),
        own_query,
        cached,
        local_heads,
        block_of,
        block_prefix,
        token_group,
        live_slots,
    )
    suffix_allowed = (
        (request_ids[:, None] == request_ids[None, :])
        & (slot_ids[None, :] <= slot_ids[:, None])
        & live_slots[:, None]
    )
    running = attend(running, own_query, own_entries[:, :, 0], own_entries[:, :, 1], suffix_allowed)
    final_max, final_total, final_sum = running
    live_grid = live_slots[:, None, None]
    safe_total = jnp.where(live_grid, final_total, 1.0)
    result = jnp.where(live_grid[..., None], final_sum / safe_total[..., None], 0.0)
    return result.astype(jnp.bfloat16).reshape(token_rows, local_heads * 2 * HEAD)


def solution(mesh):
    in_specs = (P("seq", "tp"), P("seq", "tp"), P(("seq", "tp"), None), P(), P("seq"), P("seq"))
    out_specs = P("seq", "tp")
    return jax.shard_map(
        per_device, mesh=mesh, in_specs=in_specs, out_specs=out_specs, check_vma=False
    )
```

profile of v0, /device:TPU:1, one launch (start us, length us, event | category | flops | bytes accessed | tf_op | source)
XLA Modules:
  0.0 292.7 jit_solution(12591821938182171553)
XLA Ops:
  6.5 0.7 all-gather.3.cloned.1.call-update
  7.3 150.3 %all-gather.3.cloned.1.call-done = bf16[128,4,4096]{2,1,0:T(4,128)(2,1)} async-done(((bf16[1,4,4096]{2,1,0:T(4,128)(2,1)}), bf16[128,4,4096]{2,1,0:T(4,128)(2,1)}) %all-gather.3.cloned.1.call-update) | async-done | bytes 4194320 | tf_op jit(solution)/shard_map/all_gather | solution.py:81
  157.6 7.9 %all_to_all.12 = bf16[512,4,1024]{2,1,0:T(4,128)(2,1)} reshape(bf16[128,4,4096]{2,1,0:T(4,128)(2,1)} %all-gather.3.cloned.1.call-done) | data formatting | bytes 8388608 | tf_op jit(solution)/shard_map/all_to_all | solution.py:82
  165.4 5.5 %copy.96 = bf16[512,4,1024]{2,0,1:T(8,128)(2,1)} copy(bf16[512,4,1024]{2,1,0:T(4,128)(2,1)} %all_to_all.12) | data formatting | bytes 8388608 | tf_op jit(solution)/shard_map/all_to_all | solution.py:82
  171.0 5.0 %all-to-all-start = ((bf16[512,4,1024]{2,0,1:T(8,128)(2,1)}), bf16[512,4,1024]{2,0,1:T(8,128)(2,1)}, u32[]{:S(2)}, u32[]{:S(2)}) async-start(bf16[512,4,1024]{2,0,1:T(8,128)(2,1)} %copy.96), calls=%async_computation | async-start | bytes 8388608 | tf_op jit(solution)/shard_map/all_to_all | solution.py:82
  176.2 0.6 slice.50
  177.1 0.7 iota_compare_fusion.7
  178.0 0.9 select_reduce_fusion
  179.6 89.3 %all-to-all-done = bf16[512,4,1024]{2,0,1:T(8,128)(2,1)} async-done(((bf16[512,4,1024]{2,0,1:T(8,128)(2,1)}), bf16[512,4,1024]{2,0,1:T(8,128)(2,1)}, u32[]{:S(2)}, u32[]{:S(2)}) %all-to-all-start) | async-done | bytes 4194336 | tf_op jit(solution)/shard_map/all_to_all | solution.py:82
  269.0 6.2 %copy.97 = bf16[512,4,1024]{0,2,1:T(8,128)(2,1)} copy(bf16[512,4,1024]{2,0,1:T(8,128)(2,1)} %all-to-all-done) | data formatting | bytes 8388608 | tf_op jit(solution)/shard_map/all_to_all | solution.py:82
  275.2 2.4 fusion.108
  277.6 0.5 fusion.1
  278.2 0.5 fusion.2
  278.7 0.5 fusion.3
  279.3 0.5 fusion
  279.8 0.5 fusion.4
  280.5 0.5 fusion.10
  281.0 0.5 fusion.8
  281.5 0.5 fusion.6
  282.1 0.7 fusion.19
  282.8 0.7 fusion.17
  283.4 0.7 fusion.15
  284.1 0.7 fusion.13
  285.1 0.9 copy.119
  (25 shorter events, 1.9 us)
Async XLA Ops:
  6.5 151.0 %all-gather.3.cloned.1.call-start = ((), (), s32[]{:S(2)}) async-start(), calls=%async_computation.1 | async-start | bytes 4227072 | tf_op jit(solution)/shard_map/all_gather | solution.py:81
  170.9 5.0 %copy-start.3 = (s32[4]{0:T(128)S(1)}, s32[4]{0:T(128)}, u32[]{:S(2)}) copy-start(s32[4]{0:T(128)} %param.10) | copy-start | bytes 52
  170.9 5.8 %copy-start = (bf16[128,1024]{1,0:T(8,128)(2,1)S(1)}, bf16[128,1024]{1,0:T(8,128)(2,1)}, u32[]{:S(2)}) copy-start(bf16[128,1024]{1,0:T(8,128)(2,1)} %param.6) | copy-start | bytes 786436
  170.9 6.0 %copy-start.1 = (bf16[128,1024]{1,0:T(8,128)(2,1)S(1)}, bf16[128,1024]{1,0:T(8,128)(2,1)}, u32[]{:S(2)}) copy-start(bf16[128,1024]{1,0:T(8,128)(2,1)} %param.7) | copy-start | bytes 786436
  170.9 6.9 %copy-start.4 = (s32[4]{0:T(128)S(1)}, s32[4]{0:T(128)}, u32[]{:S(2)}) copy-start(s32[4]{0:T(128)} %param.11) | copy-start | bytes 52
  171.0 7.0 %copy-start.2 = (s32[512]{0:T(512)S(1)}, s32[512]{0:T(512)}, u32[]{:S(2)}) copy-start(s32[512]{0:T(512)} %param.9) | copy-start | bytes 6148
  171.0 98.0 %all-to-all-start = ((bf16[512,4,1024]{2,0,1:T(8,128)(2,1)}), bf16[512,4,1024]{2,0,1:T(8,128)(2,1)}, u32[]{:S(2)}, u32[]{:S(2)}) async-start(bf16[512,4,1024]{2,0,1:T(8,128)(2,1)} %copy.96), calls=%async_computation | async-start | bytes 8388608 | tf_op jit(solution)/shard_map/all_to_all | solution.py:82
Sparse Core Ops, SparseCore 0:
  11.9 145.6 all-gather.2
where the time goes:
time: 293 us
  waiting for transfers between devices  240 us (82%)
  local copies, waits for them, and re-layouts  23.8 us (8%)
  between operations  13.6 us (5%)
  matrix products  5.38 us (2%)
  starting transfers between devices  5 us (2%)
  other arithmetic  4.64 us (2%)
    all_gather x1, waiting for transfers between devices, per_device(): gathered = lax.all_gather(prefix_cache, 'seq', axis=0, tiled=True)  150 us
    all_to_all x1, waiting for transfers between devices, per_device(): lax.all_to_all(gathered, 'tp', split_axis=1, concat_axis=0, tiled=True)  89.3 us
    all_to_all x3, local copies, waits for them, and re-layouts, per_device(): lax.all_to_all(gathered, 'tp', split_axis=1, concat_axis=0, tiled=True)  19.6 us
  transfers between devices with their start and end apart: 2, of which 2 were waited for; matrix products, arithmetic and copies ran while one was open for 1% of the time, Pallas kernels for 0%

commit v1 on v0

--- a/solution.py
+++ b/solution.py
@@ -8,6 +8,12 @@
 HEAD = 128
 masked_score = -1e30
 section_rows = 512
+_rest_turns = lambda raw, ax_name: jnp.concatenate(
+    lax.all_to_all(
+        jnp.stack(jnp.split(raw, lax.axis_size(ax_name), 1)), ax_name, split_axis=0, concat_axis=0
+    ),
+    0,
+)
 
 
 def token_layout(lengths, prefixes, slots):
@@ -79,7 +85,7 @@
     own_query = queries.reshape(token_rows, local_heads, 2, HEAD)
     own_entries = suffix_entries.reshape(token_rows, local_heads, 2, HEAD)
     gathered = lax.all_gather(prefix_cache, "seq", axis=0, tiled=True)
-    cached = lax.all_to_all(gathered, "tp", split_axis=1, concat_axis=0, tiled=True)
+    cached = _rest_turns(gathered, ax_name="tp")
     span = seq_count * block_rows
 
     def block_of(positions):

time: 293 us -> 294 us (level)
  local copies, waits for them, and re-layouts: 23.8 us -> 20.8 us
    all_to_all x3 -> x0, local copies, waits for them, and re-layouts: 19.6 us -> none  [per_device(): lax.all_to_all(gathered, 'tp', split_axis=1, concat_axis=0, tiled=True)]
    unnamed x11 -> x32, local copies, waits for them, and re-layouts: 0.19 us -> 8.06 us
    slice x1 -> x5, local copies, waits for them, and re-layouts: 2.44 us -> 8.56 us  [sweep(): rows[offset:offset + row_count].reshape(row_count, head_count, 2, HEAD)]
  transfers between devices with their start and end apart: 2 -> 2, of which waited for: 2 -> 2; matrix products, arithmetic and copies ran while one was open for 1% -> 2% of each run, Pallas kernels for 0% -> 0%
where the time goes in v1:
time: 294 us; the launch traced here: 293 us
  waiting for transfers between devices  238 us (81%)
  local copies, waits for them, and re-layouts  20.8 us (7%)
  between operations  13.7 us (5%)
  matrix products  7.79 us (3%)
  other arithmetic  7.44 us (3%)
  starting transfers between devices  5 us (2%)
    all_gather x1, waiting for transfers between devices, per_device(): gathered = lax.all_gather(prefix_cache, 'seq', axis=0, tiled=True)  150 us
    all_to_all x1, waiting for transfers between devices, lax.all_to_all(jnp.stack(jnp.split(raw, lax.axis_size(ax_name), 1)), ax_n...  87.4 us
    slice x5, local copies, waits for them, and re-layouts, sweep(): rows[offset:offset + row_count].reshape(row_count, head_count, 2, HEAD)  8.56 us
    unnamed x32, local copies, waits for them, and re-layouts  8.06 us
  transfers between devices with their start and end apart: 2, of which 2 were waited for; matrix products, arithmetic and copies ran while one was open for 2% of the time, Pallas kernels for 0%

profile of v1, /device:TPU:1, one launch (start us, length us, event | category | flops | bytes accessed | tf_op | source)
XLA Modules:
  0.0 293.1 jit_solution(7256748601088628219)
XLA Ops:
  6.5 0.7 all-gather.3.cloned.1.call-update
  7.3 150.3 %all-gather.3.cloned.1.call-done = bf16[128,4,4096]{2,1,0:T(4,128)(2,1)} async-done(((bf16[1,4,4096]{2,1,0:T(4,128)(2,1)}), bf16[128,4,4096]{2,1,0:T(4,128)(2,1)}) %all-gather.3.cloned.1.call-update) | async-done | bytes 4194320 | tf_op jit(solution)/shard_map/all_gather | solution.py:87
  157.6 6.9 %reshape.525 = bf16[512,4096]{1,0:T(8,128)(2,1)} reshape(bf16[128,4,4096]{2,1,0:T(4,128)(2,1)} %all-gather.3.cloned.1.call-done) | data formatting | bytes 8388608
  164.5 2.6 slice_bitcast_fusion.3
  167.1 2.2 pad_maximum_fusion
  169.4 5.0 %all-to-all-start = ((bf16[4,512,1024]{2,1,0:T(8,128)(2,1)}), bf16[4,512,1024]{2,1,0:T(8,128)(2,1)}, u32[]{:S(2)}, u32[]{:S(2)}) async-start(bf16[4,512,1024]{2,1,0:T(8,128)(2,1)} %pad_maximum_fusion), calls=%async_computation | async-start | bytes 8388608 | tf_op jit(solution)/shard_map/all_to_all | solution.py:12
  174.6 0.6 slice.50
  175.5 0.6 iota_compare_fusion.7
  176.3 0.9 select_reduce_fusion
  177.3 1.0 compare_and_fusion.2
  178.3 1.7 fusion.109
  180.1 87.4 %all-to-all-done = bf16[4,512,1024]{2,1,0:T(8,128)(2,1)} async-done(((bf16[4,512,1024]{2,1,0:T(8,128)(2,1)}), bf16[4,512,1024]{2,1,0:T(8,128)(2,1)}, u32[]{:S(2)}, u32[]{:S(2)}) %all-to-all-start) | async-done | bytes 4194336 | tf_op jit(solution)/shard_map/all_to_all | solution.py:12
  267.4 3.9 %fusion.108 = (bf16[1,512,1024]{2,1,0:T(8,128)(2,1)}, bf16[1,512,1024]{2,1,0:T(8,128)(2,1)S(1)}, bf16[1,512,1024]{2,1,0:T(8,128)(2,1)S(1)}, bf16[1,512,1024]{2,1,0:T(8,128)(2,1)S(1)}) fusion(bf16[4,512,1024]{2,1,0:T(8,128)(2,1)} %all-to-all-done), kind=kLoop, calls=%fused_computation.202 | loop fusion | bytes 8388608 | tf_op jit(solution)/shard_map/slice | solution.py:66
  271.3 2.3 copy.103
  273.6 1.3 copy.113
  275.4 0.5 copy.98
  276.0 1.6 fusion
  277.6 0.5 fusion.2
  278.1 0.6 copy-done
  282.5 0.7 fusion.19
  283.2 0.7 fusion.17
  283.8 0.7 fusion.15
  284.5 0.7 fusion.13
  285.4 0.9 copy.123
  (49 shorter events, 5.3 us)
Async XLA Ops:
  6.5 151.1 %all-gather.3.cloned.1.call-start = ((), (), s32[]{:S(2)}) async-start(), calls=%async_computation.1 | async-start | bytes 4227072 | tf_op jit(solution)/shard_map/all_gather | solution.py:87
  169.4 5.0 %copy-start.13 = (s32[4]{0:T(128)S(1)}, s32[4]{0:T(128)}, u32[]{:S(2)}) copy-start(s32[4]{0:T(128)} %param.10) | copy-start | bytes 52
  169.4 5.8 %copy-start.3 = (bf16[128,1024]{1,0:T(8,128)(2,1)S(1)}, bf16[128,1024]{1,0:T(8,128)(2,1)}, u32[]{:S(2)}) copy-start(bf16[128,1024]{1,0:T(8,128)(2,1)} %param.6) | copy-start | bytes 786436
  169.4 6.0 %copy-start.4 = (bf16[128,1024]{1,0:T(8,128)(2,1)S(1)}, bf16[128,1024]{1,0:T(8,128)(2,1)}, u32[]{:S(2)}) copy-start(bf16[128,1024]{1,0:T(8,128)(2,1)} %param.7) | copy-start | bytes 786436
  169.4 6.9 %copy-start.14 = (s32[4]{0:T(128)S(1)}, s32[4]{0:T(128)}, u32[]{:S(2)}) copy-start(s32[4]{0:T(128)} %param.11) | copy-start | bytes 52
  169.4 6.9 %copy-start.12 = (s32[512]{0:T(512)S(1)}, s32[512]{0:T(512)}, u32[]{:S(2)}) copy-start(s32[512]{0:T(512)} %param.9) | copy-start | bytes 6148
  169.4 98.0 %all-to-all-start = ((bf16[4,512,1024]{2,1,0:T(8,128)(2,1)}), bf16[4,512,1024]{2,1,0:T(8,128)(2,1)}, u32[]{:S(2)}, u32[]{:S(2)}) async-start(bf16[4,512,1024]{2,1,0:T(8,128)(2,1)} %pad_maximum_fusion), calls=%async_computation | async-start | bytes 8388608 | tf_op jit(solution)/shard_map/all_to_all | solution.py:12
  175.3 4.7 %copy-start.5 = (bf16[128,4,2,128]{3,2,1,0:T(2,128)(2,1)}, bf16[128,4,2,128]{3,2,1,0:T(2,128)(2,1)S(1)}, u32[]{:S(2)}) copy-start(bf16[128,4,2,128]{3,2,1,0:T(2,128)(2,1)S(1)} %reshape.518) | copy-start | bytes 786436
  176.1 3.9 %copy-start.9 = (pred[128]{0:T(512)(128)(4,1)}, pred[128]{0:T(512)(128)(4,1)S(1)}, u32[]{:S(2)}) copy-start(pred[128]{0:T(512)(128)(4,1)S(1)} %iota_compare_fusion.7) | copy-start | bytes 388
  276.0 1.6 copy-start.6
  277.6 1.2 copy-start
  278.1 1.3 copy-start.1
  278.1 1.3 copy-start.7
  279.3 0.7 copy-start.11
  279.3 0.9 copy-start.8
  279.4 1.3 copy-start.2
  281.4 1.1 copy-start.10
Sparse Core Ops, SparseCore 0:
  11.9 145.6 all-gather.2
